TPU v7x, 32 devices: a whole 2x2x4 slice. The times are simulated.
32 devices in a mesh: section: 2 (over x), dp: 4 (over z), mp: 4 (over y, core).
Axes of the slice: x: 2, y: 2, z: 4, core: 2. Of those that a mesh axis runs over, the one named last changes fastest.
Arguments:
- queries: bfloat16 [2, 4, 640, 4096], P('section', 'dp', None, 'mp')
- keys: bfloat16 [2, 4, 640, 4096], P('section', 'dp', None, 'mp')
- values: bfloat16 [2, 4, 640, 4096], P('section', 'dp', None, 'mp'), may hold values from -6 to 6
- grad_out: bfloat16 [2, 4, 640, 4096], P('section', 'dp', None, 'mp'), may hold values from -6 to 6
- positions: int32 [2, 4, 640], P('section', 'dp'), may hold values from 0 to 319, as said below
Outputs:
- received: bfloat16 [2, 4, 3, 640, 4096], P('section', 'dp', None, 'mp')
- bias_grad: float32 [2, 3, 4096], P('section')
Inputs may be any that keep to these rules, and one draw needn't show every extreme that they name: `positions`: along each sequence a position is 0 or one more than the position before it; the first is 0; a document starts at token 320, and none is longer than 320 tokens.
All inputs are finite; a program needn't handle non-finite values.
Results may differ from a plain program's by a relative error of at most 0.0065.
Values may be sent and summed in bfloat16 or wider, within the bound.
No kernel may reach another device: no remote copies, remote signals or barrier semaphores. Data moves between devices by JAX's collectives and lax.ppermute only.
A program may use at most 64 MiB of HBM per device.

v0:
```python
import math
import jax
import jax.numpy as jnp
from jax import lax
from jax.sharding import PartitionSpec as P

HEAD_DIM = 128
CHUNK_HEADS = 2


def chunk_grads(query_rows, key_rows, value_rows, grad_rows, allowed, halves):
    length, width = query_rows.shape
    heads = width // HEAD_DIM
    block = length // halves
    scaling = 1.0 / math.sqrt(HEAD_DIM)

    def split(rows):
        return rows.reshape(halves, block, heads, HEAD_DIM)

    q, k, v, g = (split(query_rows), split(key_rows), split(value_rows), split(grad_rows))
    scores = jnp.einsum("bqhd,bkhd->bhqk", q, k, preferred_element_type=jnp.float32) * scaling
    scores = jnp.where(allowed[:, None], scores, jnp.float32(-1e30))
    highest = jnp.max(scores, axis=-1, keepdims=True)
    expont = jnp.exp(scores - highest)
    attn = expont / jnp.sum(expont, axis=-1, keepdims=True)
    attn_low = attn.astype(jnp.bfloat16)
    grad_v = jnp.einsum("bhqk,bqhd->bkhd", attn_low, g, preferred_element_type=jnp.float32)
    grad_attn = jnp.einsum("bqhd,bkhd->bhqk", g, v, preferred_element_type=jnp.float32)
    delta = jnp.sum(attn * grad_attn, axis=-1, keepdims=True)
    grad_scores = (attn * (grad_attn - delta) * scaling).astype(jnp.bfloat16)
    grad_q = jnp.einsum("bhqk,bkhd->bqhd", grad_scores, k, preferred_element_type=jnp.float32)
    grad_k = jnp.einsum("bhqk,bqhd->bkhd", grad_scores, q, preferred_element_type=jnp.float32)
    blocks = jnp.stack([grad_q, grad_k, grad_v]).astype(jnp.bfloat16)
    return blocks.reshape(3, length, width)


def per_device(queries, keys, values, grad_out, positions):
    query_rows = queries[0, 0]
    key_rows = keys[0, 0]
    value_rows = values[0, 0]
    grad_rows = grad_out[0, 0]
    token_positions = positions[0, 0]
    length, columns = query_rows.shape
    sections = lax.axis_size("section")
    parts = lax.axis_size("mp")
    replicas = lax.axis_size("dp")
    part = lax.axis_index("mp")
    rows = length // parts
    halves = 2
    block = length // halves
    local = jnp.arange(block, dtype=jnp.int32)
    pos = token_positions.reshape(halves, block)
    allowed = (local[None, None, :] <= local[None, :, None]) & (
        local[None, None, :] >= (local[None, :] - pos)[:, :, None]
    )

    def pairs(shift):
        return [
            ((s + 1) * parts + m, s * parts + (m + shift) % parts)
            for s in range(sections - 1)
            for m in range(parts)
        ]

    width = CHUNK_HEADS * HEAD_DIM
    chunk_count = columns // width
    arrived = [[None] * chunk_count for _ in range(parts)]
    sums = []
    for c in range(chunk_count):
        cols = slice(c * width, (c + 1) * width)
        grads = chunk_grads(
            query_rows[:, cols],
            key_rows[:, cols],
            value_rows[:, cols],
            grad_rows[:, cols],
            allowed,
            halves,
        )
        sums.append(jnp.sum(grads.astype(jnp.float32), axis=1))
        for shift in range(parts):
            target = (part + shift) % parts
            piece = lax.dynamic_slice_in_dim(grads, target * rows, rows, 1)
            arrived[shift][c] = lax.ppermute(piece, ("section", "mp"), pairs(shift))
    own = jnp.concatenate(sums, axis=1)
    slots = lax.dynamic_update_slice_in_dim(
        jnp.zeros((3, columns * parts), jnp.float32), own, part * columns, 1
    )
    totals = lax.psum(slots, ("dp", "mp"))
    totals = lax.ppermute(totals, "section", [(s + 1, s) for s in range(sections - 1)])
    bias_grad = totals / math.sqrt(replicas * length)
    received = jnp.zeros((3, rows, columns * parts), jnp.bfloat16)
    for shift in range(parts):
        source = (part - shift) % parts
        piece = jnp.concatenate(arrived[shift], axis=2)
        received = lax.dynamic_update_slice_in_dim(received, piece, source * columns, 2)
    return (received[None, None], bias_grad[None])


def solution(mesh):
    return jax.shard_map(
        per_device,
        mesh=mesh,
        in_specs=(
            P("section", "dp", None, "mp"),
            P("section", "dp", None, "mp"),
            P("section", "dp", None, "mp"),
            P("section", "dp", None, "mp"),
            P("section", "dp", None),
        ),
        out_specs=(P("section", "dp", None, "mp", None), P("section", None, None)),
        check_vma=False,
    )
```

profile of v0, /device:TPU:5, one launch (start us, length us, event | category | flops | bytes accessed | tf_op | source)
XLA Modules:
  0.0 251.5 jit_solution(15631880437137905530)
XLA Ops:
  12.1 3.2 %fusion.256 = (f32[2,2,320]{2,1,0:T(2,128)S(1)}, f32[2,2,320,320]{2,3,1,0:T(8,128)}) fusion(pred[2,320,320]{1,2,0:T(8,128)(4,1)S(1)} %fusion.124, bf16[2,320,2,128]{3,2,1,0:T(2,128)(2,1)} %reshape.143, bf16[2,320,2,128]{3,2,1,0:T(2,128)(2,1)} %reshape.142), kind=kOutput, calls=%fused_computation.205 | convolution fusion | flops 106496320 | bytes 2503680 | tf_op jit(solution)/shard_map/sub | solution.py:24
  15.3 3.8 %fusion.75 = bf16[2,320,2,128]{3,1,2,0:T(8,128)(2,1)} fusion(f32[2,2,320,320]{2,3,1,0:T(8,128)S(1)} %fusion.135, bf16[2,320,2,128]{3,2,1,0:T(2,128)(2,1)} %reshape.143, f32[2,2,320,320]{2,3,1,0:T(8,128)} %get-tuple-element.41, f32[2,2,320]{2,1,0:T(2,128)S(1)} %get-tuple-element.40), kind=kOutput, calls=%fused_computation.57 | convolution fusion | flops 107890240 | bytes 3937280 | tf_op jit(solution)/shard_map/bhqk,bkhd->bqhd/dot_general | solution.py:31
  19.0 3.6 %fusion.72 = bf16[2,320,2,128]{3,1,2,0:T(8,128)(2,1)} fusion(f32[2,2,320,320]{2,3,1,0:T(8,128)S(1)} %fusion.135, bf16[2,320,2,128]{3,2,1,0:T(2,128)(2,1)} %reshape.142, f32[2,2,320,320]{2,3,1,0:T(8,128)} %get-tuple-element.41, f32[2,2,320]{2,1,0:T(2,128)S(1)} %get-tuple-element.40), kind=kOutput, calls=%fused_computation.56 | convolution fusion | flops 107890240 | bytes 3937280 | tf_op jit(solution)/shard_map/bhqk,bqhd->bkhd/dot_general | solution.py:32
  22.7 2.8 %fusion.96 = bf16[2,320,2,128]{3,1,2,0:T(8,128)(2,1)} fusion(bf16[2,320,2,128]{3,2,1,0:T(2,128)(2,1)} %reshape.144, f32[2,2,320,320]{2,3,1,0:T(8,128)} %get-tuple-element.41, f32[2,2,320]{2,1,0:T(2,128)S(1)} %get-tuple-element.40), kind=kOutput, calls=%fused_computation.64 | convolution fusion | flops 105840640 | bytes 2298880 | tf_op jit(solution)/shard_map/bhqk,bqhd->bkhd/dot_general | solution.py:27
  30.9 3.8 %fusion.81 = bf16[2,320,2,128]{3,1,2,0:T(8,128)(2,1)} fusion(f32[2,2,320,320]{2,3,1,0:T(8,128)S(1)} %fusion.133, bf16[2,320,2,128]{3,2,1,0:T(2,128)(2,1)} %copy-done.22, f32[2,2,320,320]{2,3,1,0:T(8,128)} %get-tuple-element.39, f32[2,2,320]{2,1,0:T(2,128)S(1)} %get-tuple-element.38), kind=kOutput, calls=%fused_computation.59 | convolution fusion | flops 107890240 | bytes 3937280 | tf_op jit(solution)/shard_map/bhqk,bkhd->bqhd/dot_general | solution.py:31
  34.7 3.6 %fusion.78 = bf16[2,320,2,128]{3,1,2,0:T(8,128)(2,1)} fusion(f32[2,2,320,320]{2,3,1,0:T(8,128)S(1)} %fusion.133, bf16[2,320,2,128]{3,2,1,0:T(2,128)(2,1)} %copy-done.20, f32[2,2,320,320]{2,3,1,0:T(8,128)} %get-tuple-element.39, f32[2,2,320]{2,1,0:T(2,128)S(1)} %get-tuple-element.38), kind=kOutput, calls=%fused_computation.58 | convolution fusion | flops 107890240 | bytes 3937280 | tf_op jit(solution)/shard_map/bhqk,bqhd->bkhd/dot_general | solution.py:32
  38.3 2.8 %fusion.97 = bf16[2,320,2,128]{3,1,2,0:T(8,128)(2,1)} fusion(bf16[2,320,2,128]{3,2,1,0:T(2,128)(2,1)} %reshape.148, f32[2,2,320,320]{2,3,1,0:T(8,128)} %get-tuple-element.39, f32[2,2,320]{2,1,0:T(2,128)S(1)} %get-tuple-element.38), kind=kOutput, calls=%fused_computation.65 | convolution fusion | flops 105840640 | bytes 2298880 | tf_op jit(solution)/shard_map/bhqk,bqhd->bkhd/dot_general | solution.py:27
  46.6 3.8 %fusion.87 = bf16[2,320,2,128]{3,1,2,0:T(8,128)(2,1)} fusion(f32[2,2,320,320]{2,3,1,0:T(8,128)S(1)} %fusion.131, bf16[2,320,2,128]{3,2,1,0:T(2,128)(2,1)} %copy-done.23, f32[2,2,320,320]{2,3,1,0:T(8,128)} %get-tuple-element.37, f32[2,2,320]{2,1,0:T(2,128)S(1)} %get-tuple-element.36), kind=kOutput, calls=%fused_computation.61 | convolution fusion | flops 107890240 | bytes 3937280 | tf_op jit(solution)/shard_map/bhqk,bkhd->bqhd/dot_general | solution.py:31
  50.4 3.6 %fusion.84 = bf16[2,320,2,128]{3,1,2,0:T(8,128)(2,1)} fusion(f32[2,2,320,320]{2,3,1,0:T(8,128)S(1)} %fusion.131, bf16[2,320,2,128]{3,2,1,0:T(2,128)(2,1)} %copy-done.21, f32[2,2,320,320]{2,3,1,0:T(8,128)} %get-tuple-element.37, f32[2,2,320]{2,1,0:T(2,128)S(1)} %get-tuple-element.36), kind=kOutput, calls=%fused_computation.60 | convolution fusion | flops 107890240 | bytes 3937280 | tf_op jit(solution)/shard_map/bhqk,bqhd->bkhd/dot_general | solution.py:32
  59.8 3.6 %fusion.90 = bf16[2,320,2,128]{3,1,2,0:T(8,128)(2,1)} fusion(f32[2,2,320,320]{2,3,1,0:T(8,128)S(1)} %fusion.129, bf16[2,320,2,128]{3,2,1,0:T(2,128)(2,1)S(1)} %reshape.154, f32[2,2,320,320]{2,3,1,0:T(8,128)} %get-tuple-element.35, f32[2,2,320]{2,1,0:T(2,128)S(1)} %get-tuple-element.34), kind=kOutput, calls=%fused_computation.62 | convolution fusion | flops 107890240 | bytes 3937280 | tf_op jit(solution)/shard_map/bhqk,bqhd->bkhd/dot_general | solution.py:32
  63.4 3.7 %fusion.93 = bf16[2,320,2,128]{3,1,2,0:T(8,128)(2,1)} fusion(f32[2,2,320,320]{2,3,1,0:T(8,128)S(1)} %fusion.129, bf16[2,320,2,128]{3,2,1,0:T(2,128)(2,1)S(1)} %reshape.155, f32[2,2,320,320]{2,3,1,0:T(8,128)} %get-tuple-element.35, f32[2,2,320]{2,1,0:T(2,128)S(1)} %get-tuple-element.34), kind=kOutput, calls=%fused_computation.63 | convolution fusion | flops 107890240 | bytes 3937280 | tf_op jit(solution)/shard_map/bhqk,bkhd->bqhd/dot_general | solution.py:31
  67.1 2.7 %fusion.99 = bf16[2,320,2,128]{3,1,2,0:T(8,128)(2,1)} fusion(bf16[2,320,2,128]{3,2,1,0:T(2,128)(2,1)S(1)} %reshape.156, f32[2,2,320,320]{2,3,1,0:T(8,128)} %get-tuple-element.35, f32[2,2,320]{2,1,0:T(2,128)S(1)} %get-tuple-element.34), kind=kOutput, calls=%fused_computation.67 | convolution fusion | flops 105840640 | bytes 2298880 | tf_op jit(solution)/shard_map/bhqk,bqhd->bkhd/dot_general | solution.py:27
  99.6 53.4 %psum.7 = f32[3,4096]{1,0:T(4,128)} all-reduce(f32[3,4096]{1,0:T(4,128)S(1)} %maximum_dynamic-update-slice_fusion), channel_id=1, replica_groups=mesh['section'=2,'dp'=4,'mp'=4] {'dp','mp'}, use_global_device_ids=true, to_apply=%region_16.17 | all-reduce | flops 12288 | bytes 98304 | tf_op jit(solution)/shard_map/psum | solution.py:87
  168.7 4.0 %collective-permute-done.2 = bf16[3,160,256]{2,1,0:T(8,128)(2,1)S(1)} collective-permute-done((bf16[3,160,256]{2,1,0:T(8,128)(2,1)}, bf16[3,160,256]{2,1,0:T(8,128)(2,1)S(1)}, u32[]{:S(2)}, u32[]{:S(2)}) %collective-permute-start.2) | collective-permute-done | bytes 245792 | tf_op jit(solution)/shard_map/ppermute | solution.py:82
  174.0 3.9 %collective-permute-done.3 = bf16[3,160,256]{2,1,0:T(8,128)(2,1)S(1)} collective-permute-done((bf16[3,160,256]{2,1,0:T(8,128)(2,1)}, bf16[3,160,256]{2,1,0:T(8,128)(2,1)S(1)}, u32[]{:S(2)}, u32[]{:S(2)}) %collective-permute-start.3) | collective-permute-done | bytes 245792 | tf_op jit(solution)/shard_map/ppermute | solution.py:82
  179.1 12.5 %collective-permute-done.4 = bf16[3,160,256]{2,1,0:T(8,128)(2,1)S(1)} collective-permute-done((bf16[3,160,256]{2,1,0:T(8,128)(2,1)}, bf16[3,160,256]{2,1,0:T(8,128)(2,1)S(1)}, u32[]{:S(2)}, u32[]{:S(2)}) %collective-permute-start.4) | collective-permute-done | bytes 245792 | tf_op jit(solution)/shard_map/ppermute | solution.py:82
  193.0 4.0 %collective-permute-done.5 = bf16[3,160,256]{2,1,0:T(8,128)(2,1)S(1)} collective-permute-done((bf16[3,160,256]{2,1,0:T(8,128)(2,1)}, bf16[3,160,256]{2,1,0:T(8,128)(2,1)S(1)}, u32[]{:S(2)}, u32[]{:S(2)}) %collective-permute-start.5) | collective-permute-done | bytes 245792 | tf_op jit(solution)/shard_map/ppermute | solution.py:82
  198.9 3.3 %collective-permute-done.6 = bf16[3,160,256]{2,1,0:T(8,128)(2,1)S(1)} collective-permute-done((bf16[3,160,256]{2,1,0:T(8,128)(2,1)S(1)}, bf16[3,160,256]{2,1,0:T(8,128)(2,1)S(1)}, u32[]{:S(2)}, u32[]{:S(2)}) %collective-permute-start.6) | collective-permute-done | bytes 245792 | tf_op jit(solution)/shard_map/ppermute | solution.py:82
  209.8 4.1 %collective-permute-done.9 = bf16[3,160,256]{2,1,0:T(8,128)(2,1)S(1)} collective-permute-done((bf16[3,160,256]{2,1,0:T(8,128)(2,1)S(1)}, bf16[3,160,256]{2,1,0:T(8,128)(2,1)S(1)}, u32[]{:S(2)}, u32[]{:S(2)}) %collective-permute-start.9) | collective-permute-done | bytes 245792 | tf_op jit(solution)/shard_map/ppermute | solution.py:82
  215.1 4.0 %collective-permute-done.10 = bf16[3,160,256]{2,1,0:T(8,128)(2,1)S(1)} collective-permute-done((bf16[3,160,256]{2,1,0:T(8,128)(2,1)S(1)}, bf16[3,160,256]{2,1,0:T(8,128)(2,1)S(1)}, u32[]{:S(2)}, u32[]{:S(2)}) %collective-permute-start.10) | collective-permute-done | bytes 245792 | tf_op jit(solution)/shard_map/ppermute | solution.py:82
  220.5 3.9 %collective-permute-done.11 = bf16[3,160,256]{2,1,0:T(8,128)(2,1)S(1)} collective-permute-done((bf16[3,160,256]{2,1,0:T(8,128)(2,1)S(1)}, bf16[3,160,256]{2,1,0:T(8,128)(2,1)S(1)}, u32[]{:S(2)}, u32[]{:S(2)}) %collective-permute-start.11) | collective-permute-done | bytes 245792 | tf_op jit(solution)/shard_map/ppermute | solution.py:82
  224.5 13.4 %collective-permute-done.12 = bf16[3,160,256]{2,1,0:T(8,128)(2,1)S(1)} collective-permute-done((bf16[3,160,256]{2,1,0:T(8,128)(2,1)S(1)}, bf16[3,160,256]{2,1,0:T(8,128)(2,1)S(1)}, u32[]{:S(2)}, u32[]{:S(2)}) %collective-permute-start.12) | collective-permute-done | bytes 245792 | tf_op jit(solution)/shard_map/ppermute | solution.py:82
  237.9 5.3 %collective-permute-done.13 = bf16[3,160,256]{2,1,0:T(8,128)(2,1)S(1)} collective-permute-done((bf16[3,160,256]{2,1,0:T(8,128)(2,1)S(1)}, bf16[3,160,256]{2,1,0:T(8,128)(2,1)S(1)}, u32[]{:S(2)}, u32[]{:S(2)}) %collective-permute-start.13) | collective-permute-done | bytes 245792 | tf_op jit(solution)/shard_map/ppermute | solution.py:82
  243.2 3.6 %collective-permute-done.14 = bf16[3,160,256]{2,1,0:T(8,128)(2,1)S(1)} collective-permute-done((bf16[3,160,256]{2,1,0:T(8,128)(2,1)S(1)}, bf16[3,160,256]{2,1,0:T(8,128)(2,1)S(1)}, u32[]{:S(2)}, u32[]{:S(2)}) %collective-permute-start.14) | collective-permute-done | bytes 245792 | tf_op jit(solution)/shard_map/ppermute | solution.py:82
  (163 shorter events, 93.8 us)
Async XLA Ops:
  0.6 3.2 %copy-start.10 = (bf16[1,1,640,1024]{3,2,1,0:T(8,128)(2,1)S(1)}, bf16[1,1,640,1024]{3,2,1,0:T(8,128)(2,1)}, u32[]{:S(2)}) copy-start(bf16[1,1,640,1024]{3,2,1,0:T(8,128)(2,1)} %param.6) | copy-start | bytes 3932164
  4.8 3.9 %copy-start.11 = (bf16[1,1,640,1024]{3,2,1,0:T(8,128)(2,1)S(1)}, bf16[1,1,640,1024]{3,2,1,0:T(8,128)(2,1)}, u32[]{:S(2)}) copy-start(bf16[1,1,640,1024]{3,2,1,0:T(8,128)(2,1)} %param.7) | copy-start | bytes 3932164
  22.7 3.0 %copy-start.8 = (bf16[640,256]{1,0:T(8,128)(2,1)S(1)}, bf16[640,256]{1,0:T(8,128)(2,1)}, u32[]{:S(2)}) copy-start(bf16[640,256]{1,0:T(8,128)(2,1)} %get-tuple-element.13) | copy-start | bytes 983044
  38.3 3.0 %copy-start.4 = (bf16[640,256]{1,0:T(8,128)(2,1)S(1)}, bf16[640,256]{1,0:T(8,128)(2,1)}, u32[]{:S(2)}) copy-start(bf16[640,256]{1,0:T(8,128)(2,1)} %get-tuple-element.12) | copy-start | bytes 983044
  152.9 10.2 %collective-permute-start.16 = (f32[3,4096]{1,0:T(4,128)}, f32[3,4096]{1,0:T(4,128)S(1)}, u32[]{:S(2)}, u32[]{:S(2)}) collective-permute-start(f32[3,4096]{1,0:T(4,128)} %psum.7), channel_id=1, source_target_pairs={{16,0},{17,1},{18,2},{19,3},{20,4},{21,5},{22,6},{23,7},{24,8},{25... | collective-permute-start | bytes 147464 | tf_op jit(solution)/shard_map/ppermute | solution.py:88
  155.1 6.0 %copy-start = (bf16[3,640,256]{2,1,0:T(8,128)(2,1)S(1)}, bf16[3,640,256]{2,1,0:T(8,128)(2,1)}, u32[]{:S(2)}) copy-start(bf16[3,640,256]{2,1,0:T(8,128)(2,1)} %constant_dynamic-update-slice_fusion.9) | copy-start | bytes 2949124
  155.1 9.4 %collective-permute-start = (bf16[3,160,256]{2,1,0:T(8,128)(2,1)S(1)}, bf16[3,160,256]{2,1,0:T(8,128)(2,1)}, u32[]{:S(2)}, u32[]{:S(2)}) collective-permute-start(bf16[3,160,256]{2,1,0:T(8,128)(2,1)S(1)} %get-tuple-element.21), channel_id=1, source_target_pairs={{16,0},{17,1},{18,2},{19,3},{20,4},{21,5},{22,6},{23,7},{24,8},{25... | collective-permute-start | bytes 737288 | tf_op jit(solution)/shard_map/ppermute | solution.py:82
  157.4 34.3 %copy-start.24 = (bf16[3,160,256]{2,1,0:T(8,128)(2,1)S(1)}, bf16[3,160,256]{2,1,0:T(8,128)(2,1)}, u32[]{:S(2)}) copy-start(bf16[3,160,256]{2,1,0:T(8,128)(2,1)} %get-tuple-element.23) | copy-start | bytes 737284
  157.4 10.0 %collective-permute-start.1 = (bf16[3,160,256]{2,1,0:T(8,128)(2,1)}, bf16[3,160,256]{2,1,0:T(8,128)(2,1)}, u32[]{:S(2)}, u32[]{:S(2)}) collective-permute-start(bf16[3,160,256]{2,1,0:T(8,128)(2,1)} %get-tuple-element.25), channel_id=1, source_target_pairs={{16,0},{17,1},{18,2},{19,3},{20,4},{21,5},{22,6},{23,7},{24,8},{25... | collective-permute-start | bytes 737288 | tf_op jit(solution)/shard_map/ppermute | solution.py:82
  159.7 7.7 %copy-start.25 = (bf16[3,160,256]{2,1,0:T(8,128)(2,1)S(1)}, bf16[3,160,256]{2,1,0:T(8,128)(2,1)}, u32[]{:S(2)}) copy-start(bf16[3,160,256]{2,1,0:T(8,128)(2,1)} %get-tuple-element.28) | copy-start | bytes 737284
  159.7 13.0 %collective-permute-start.2 = (bf16[3,160,256]{2,1,0:T(8,128)(2,1)}, bf16[3,160,256]{2,1,0:T(8,128)(2,1)S(1)}, u32[]{:S(2)}, u32[]{:S(2)}) collective-permute-start(bf16[3,160,256]{2,1,0:T(8,128)(2,1)} %get-tuple-element.29), channel_id=1, source_target_pairs={{16,0},{17,1},{18,2},{19,3},{20,4},{21,5},{22,6},{23,7},{24,8},{25... | collective-permute-start | bytes 737288 | tf_op jit(solution)/shard_map/ppermute | solution.py:82
  161.9 16.0 %collective-permute-start.3 = (bf16[3,160,256]{2,1,0:T(8,128)(2,1)}, bf16[3,160,256]{2,1,0:T(8,128)(2,1)S(1)}, u32[]{:S(2)}, u32[]{:S(2)}) collective-permute-start(bf16[3,160,256]{2,1,0:T(8,128)(2,1)} %get-tuple-element.33), channel_id=1, source_target_pairs={{16,0},{17,1},{18,2},{19,3},{20,4},{21,5},{22,6},{23,7},{24,8},{25... | collective-permute-start | bytes 737288 | tf_op jit(solution)/shard_map/ppermute | solution.py:82
  163.2 28.5 %collective-permute-start.4 = (bf16[3,160,256]{2,1,0:T(8,128)(2,1)}, bf16[3,160,256]{2,1,0:T(8,128)(2,1)S(1)}, u32[]{:S(2)}, u32[]{:S(2)}) collective-permute-start(bf16[3,160,256]{2,1,0:T(8,128)(2,1)} %get-tuple-element.20), channel_id=1, source_target_pairs={{16,1},{17,2},{18,3},{19,0},{20,5},{21,6},{22,7},{23,4},{24,9},{25... | collective-permute-start | bytes 737288 | tf_op jit(solution)/shard_map/ppermute | solution.py:82
  164.5 32.4 %collective-permute-start.5 = (bf16[3,160,256]{2,1,0:T(8,128)(2,1)}, bf16[3,160,256]{2,1,0:T(8,128)(2,1)S(1)}, u32[]{:S(2)}, u32[]{:S(2)}) collective-permute-start(bf16[3,160,256]{2,1,0:T(8,128)(2,1)} %get-tuple-element.24), channel_id=1, source_target_pairs={{16,1},{17,2},{18,3},{19,0},{20,5},{21,6},{22,7},{23,4},{24,9},{25... | collective-permute-start | bytes 737288 | tf_op jit(solution)/shard_map/ppermute | solution.py:82
  167.4 34.8 %collective-permute-start.6 = (bf16[3,160,256]{2,1,0:T(8,128)(2,1)S(1)}, bf16[3,160,256]{2,1,0:T(8,128)(2,1)S(1)}, u32[]{:S(2)}, u32[]{:S(2)}) collective-permute-start(bf16[3,160,256]{2,1,0:T(8,128)(2,1)S(1)} %copy-done.25), channel_id=1, source_target_pairs={{16,1},{17,2},{18,3},{19,0},{20,5},{21,6},{22,7},{23,4},{24,9},{25... | collective-permute-start | bytes 737288 | tf_op jit(solution)/shard_map/ppermute | solution.py:82
  172.7 34.5 %collective-permute-start.7 = (bf16[3,160,256]{2,1,0:T(8,128)(2,1)S(1)}, bf16[3,160,256]{2,1,0:T(8,128)(2,1)S(1)}, u32[]{:S(2)}, u32[]{:S(2)}) collective-permute-start(bf16[3,160,256]{2,1,0:T(8,128)(2,1)S(1)} %get-tuple-element.32), channel_id=1, source_target_pairs={{16,1},{17,2},{18,3},{19,0},{20,5},{21,6},{22,7},{23,4},{24,9},{25... | collective-permute-start | bytes 737288 | tf_op jit(solution)/shard_map/ppermute | solution.py:82
  177.8 30.6 %collective-permute-start.8 = (bf16[3,160,256]{2,1,0:T(8,128)(2,1)S(1)}, bf16[3,160,256]{2,1,0:T(8,128)(2,1)S(1)}, u32[]{:S(2)}, u32[]{:S(2)}) collective-permute-start(bf16[3,160,256]{2,1,0:T(8,128)(2,1)S(1)} %get-tuple-element.19), channel_id=1, source_target_pairs={{16,2},{17,3},{18,0},{19,1},{20,6},{21,7},{22,4},{23,5},{24,10},{2... | collective-permute-start | bytes 737288 | tf_op jit(solution)/shard_map/ppermute | solution.py:82
  191.7 22.2 %collective-permute-start.9 = (bf16[3,160,256]{2,1,0:T(8,128)(2,1)S(1)}, bf16[3,160,256]{2,1,0:T(8,128)(2,1)S(1)}, u32[]{:S(2)}, u32[]{:S(2)}) collective-permute-start(bf16[3,160,256]{2,1,0:T(8,128)(2,1)S(1)} %copy-done.24), channel_id=1, source_target_pairs={{16,2},{17,3},{18,0},{19,1},{20,6},{21,7},{22,4},{23,5},{24,10},{2... | collective-permute-start | bytes 737288 | tf_op jit(solution)/shard_map/ppermute | solution.py:82
  196.9 22.2 %collective-permute-start.10 = (bf16[3,160,256]{2,1,0:T(8,128)(2,1)S(1)}, bf16[3,160,256]{2,1,0:T(8,128)(2,1)S(1)}, u32[]{:S(2)}, u32[]{:S(2)}) collective-permute-start(bf16[3,160,256]{2,1,0:T(8,128)(2,1)S(1)} %get-tuple-element.27), channel_id=1, source_target_pairs={{16,2},{17,3},{18,0},{19,1},{20,6},{21,7},{22,4},{23,5},{24,10},{2... | collective-permute-start | bytes 737288 | tf_op jit(solution)/shard_map/ppermute | solution.py:82
  202.2 22.2 %collective-permute-start.11 = (bf16[3,160,256]{2,1,0:T(8,128)(2,1)S(1)}, bf16[3,160,256]{2,1,0:T(8,128)(2,1)S(1)}, u32[]{:S(2)}, u32[]{:S(2)}) collective-permute-start(bf16[3,160,256]{2,1,0:T(8,128)(2,1)S(1)} %get-tuple-element.31), channel_id=1, source_target_pairs={{16,2},{17,3},{18,0},{19,1},{20,6},{21,7},{22,4},{23,5},{24,10},{2... | collective-permute-start | bytes 737288 | tf_op jit(solution)/shard_map/ppermute | solution.py:82
  207.2 30.7 %collective-permute-start.12 = (bf16[3,160,256]{2,1,0:T(8,128)(2,1)S(1)}, bf16[3,160,256]{2,1,0:T(8,128)(2,1)S(1)}, u32[]{:S(2)}, u32[]{:S(2)}) collective-permute-start(bf16[3,160,256]{2,1,0:T(8,128)(2,1)S(1)} %get-tuple-element.18), channel_id=1, source_target_pairs={{16,3},{17,0},{18,1},{19,2},{20,7},{21,4},{22,5},{23,6},{24,11},{2... | collective-permute-start | bytes 737288 | tf_op jit(solution)/shard_map/ppermute | solution.py:82
  208.5 34.7 %collective-permute-start.13 = (bf16[3,160,256]{2,1,0:T(8,128)(2,1)S(1)}, bf16[3,160,256]{2,1,0:T(8,128)(2,1)S(1)}, u32[]{:S(2)}, u32[]{:S(2)}) collective-permute-start(bf16[3,160,256]{2,1,0:T(8,128)(2,1)S(1)} %get-tuple-element.22), channel_id=1, source_target_pairs={{16,3},{17,0},{18,1},{19,2},{20,7},{21,4},{22,5},{23,6},{24,11},{2... | collective-permute-start | bytes 737288 | tf_op jit(solution)/shard_map/ppermute | solution.py:82
  213.8 33.0 %collective-permute-start.14 = (bf16[3,160,256]{2,1,0:T(8,128)(2,1)S(1)}, bf16[3,160,256]{2,1,0:T(8,128)(2,1)S(1)}, u32[]{:S(2)}, u32[]{:S(2)}) collective-permute-start(bf16[3,160,256]{2,1,0:T(8,128)(2,1)S(1)} %get-tuple-element.26), channel_id=1, source_target_pairs={{16,3},{17,0},{18,1},{19,2},{20,7},{21,4},{22,5},{23,6},{24,11},{2... | collective-permute-start | bytes 737288 | tf_op jit(solution)/shard_map/ppermute | solution.py:82
  219.1 30.3 %collective-permute-start.15 = (bf16[3,160,256]{2,1,0:T(8,128)(2,1)S(1)}, bf16[3,160,256]{2,1,0:T(8,128)(2,1)S(1)}, u32[]{:S(2)}, u32[]{:S(2)}) collective-permute-start(bf16[3,160,256]{2,1,0:T(8,128)(2,1)S(1)} %get-tuple-element.30), channel_id=1, source_target_pairs={{16,3},{17,0},{18,1},{19,2},{20,7},{21,4},{22,5},{23,6},{24,11},{2... | collective-permute-start | bytes 737288 | tf_op jit(solution)/shard_map/ppermute | solution.py:82
  (20 other events, 35.7 us)
where the time goes:
time: 253 us; the launch traced here: 251 us
  waiting for transfers between devices  68.1 us (27%)
  matrix products  55.1 us (22%)
  blocking collectives  53.4 us (21%)
  local copies, waits for them, and re-layouts  47.7 us (19%)
  starting transfers between devices  22.2 us (9%)
  other arithmetic  3.64 us (1%)
    ppermute x16, waiting for transfers between devices, per_device(): arrived[shift][c] = lax.ppermute(piece, ('section', 'mp'), pairs(shift))  68.1 us
    psum x1, blocking collectives, per_device(): totals = lax.psum(slots, ('dp', 'mp'))  53.4 us
    ppermute x16, starting transfers between devices, per_device(): arrived[shift][c] = lax.ppermute(piece, ('section', 'mp'), pairs(shift))  20.9 us
    dot_general x4, matrix products, chunk_grads(): jnp.einsum('bhqk,bkhd->bqhd', grad_scores, k, preferred_element_type=jnp....  15.1 us
    dot_general x4, matrix products, chunk_grads(): jnp.einsum('bhqk,bqhd->bkhd', grad_scores, q, preferred_element_type=jnp....  14.5 us
    another operation x16, local copies, waits for them, and re-layouts, chunk_grads(): blocks = jnp.stack([grad_q, grad_k, grad_v]).astype(jnp.bfloat16)  12.4 us
    dot_general x4, matrix products, chunk_grads(): jnp.einsum('bhqk,bqhd->bkhd', attn_low, g, preferred_element_type=jnp.flo...  11 us
    sub x4, matrix products, chunk_grads(): expont = jnp.exp(scores - highest)  9.71 us
  transfers between devices with their start and end apart: 17, of which 14 were waited for; matrix products, arithmetic and copies ran while one was open for 2% of the time, Pallas kernels for 0%

commit v1 on v0

--- a/solution.py
+++ b/solution.py
@@ -84,7 +84,7 @@
     slots = lax.dynamic_update_slice_in_dim(
         jnp.zeros((3, columns * parts), jnp.float32), own, part * columns, 1
     )
-    totals = lax.psum(slots, ("dp", "mp"))
+    totals = jnp.sum(lax.all_gather(slots, ("dp", "mp")), axis=0)
     totals = lax.ppermute(totals, "section", [(s + 1, s) for s in range(sections - 1)])
     bias_grad = totals / math.sqrt(replicas * length)
     received = jnp.zeros((3, rows, columns * parts), jnp.bfloat16)

time: 253 us -> 223 us (0.88)
  blocking collectives: 53.4 us -> 22.9 us
    psum x1 -> x0, blocking collectives: 53.4 us -> none  [per_device(): totals = lax.psum(slots, ('dp', 'mp'))]
    all_gather x0 -> x1, blocking collectives: none -> 22.9 us  [per_device(): totals = jnp.sum(lax.all_gather(slots, ('dp', 'mp')), axis=0)]
  transfers between devices with their start and end apart: 17 -> 17, of which waited for: 14 -> 16; matrix products, arithmetic and copies ran while one was open for 2% -> 3% of each run, Pallas kernels for 0% -> 0%
where the time goes in v1:
time: 223 us; the launch traced here: 221 us
  waiting for transfers between devices  65.8 us (30%)
  matrix products  55.1 us (25%)
  local copies, waits for them, and re-layouts  47.7 us (21%)
  blocking collectives  22.9 us (10%)
  starting transfers between devices  22.2 us (10%)
  other arithmetic  5.87 us (3%)
    ppermute x16, waiting for transfers between devices, per_device(): arrived[shift][c] = lax.ppermute(piece, ('section', 'mp'), pairs(shift))  65.7 us
    all_gather x1, blocking collectives, per_device(): totals = jnp.sum(lax.all_gather(slots, ('dp', 'mp')), axis=0)  22.9 us
    ppermute x16, starting transfers between devices, per_device(): arrived[shift][c] = lax.ppermute(piece, ('section', 'mp'), pairs(shift))  20.9 us
    dot_general x4, matrix products, chunk_grads(): jnp.einsum('bhqk,bkhd->bqhd', grad_scores, k, preferred_element_type=jnp....  15.1 us
    dot_general x4, matrix products, chunk_grads(): jnp.einsum('bhqk,bqhd->bkhd', grad_scores, q, preferred_element_type=jnp....  14.5 us
    another operation x16, local copies, waits for them, and re-layouts, chunk_grads(): blocks = jnp.stack([grad_q, grad_k, grad_v]).astype(jnp.bfloat16)  12.4 us
    dot_general x4, matrix products, chunk_grads(): jnp.einsum('bhqk,bqhd->bkhd', attn_low, g, preferred_element_type=jnp.flo...  11 us
    sub x4, matrix products, chunk_grads(): expont = jnp.exp(scores - highest)  9.71 us
  transfers between devices with their start and end apart: 17, of which 16 were waited for; matrix products, arithmetic and copies ran while one was open for 3% of the time, Pallas kernels for 0%

profile of v1, /device:TPU:5, one launch (start us, length us, event | category | flops | bytes accessed | tf_op | source)
XLA Modules:
  0.0 220.9 jit_solution(6214539981801723096)
XLA Ops:
  12.1 3.2 %fusion.257 = (f32[2,2,320]{2,1,0:T(2,128)S(1)}, f32[2,2,320,320]{2,3,1,0:T(8,128)}) fusion(pred[2,320,320]{1,2,0:T(8,128)(4,1)S(1)} %fusion.124, bf16[2,320,2,128]{3,2,1,0:T(2,128)(2,1)} %reshape.145, bf16[2,320,2,128]{3,2,1,0:T(2,128)(2,1)} %reshape.144), kind=kOutput, calls=%fused_computation.206 | convolution fusion | flops 106496320 | bytes 2503680 | tf_op jit(solution)/shard_map/sub | solution.py:24
  15.3 3.8 %fusion.75 = bf16[2,320,2,128]{3,1,2,0:T(8,128)(2,1)} fusion(f32[2,2,320,320]{2,3,1,0:T(8,128)S(1)} %fusion.135, bf16[2,320,2,128]{3,2,1,0:T(2,128)(2,1)} %reshape.145, f32[2,2,320,320]{2,3,1,0:T(8,128)} %get-tuple-element.41, f32[2,2,320]{2,1,0:T(2,128)S(1)} %get-tuple-element.40), kind=kOutput, calls=%fused_computation.57 | convolution fusion | flops 107890240 | bytes 3937280 | tf_op jit(solution)/shard_map/bhqk,bkhd->bqhd/dot_general | solution.py:31
  19.0 3.6 %fusion.72 = bf16[2,320,2,128]{3,1,2,0:T(8,128)(2,1)} fusion(f32[2,2,320,320]{2,3,1,0:T(8,128)S(1)} %fusion.135, bf16[2,320,2,128]{3,2,1,0:T(2,128)(2,1)} %reshape.144, f32[2,2,320,320]{2,3,1,0:T(8,128)} %get-tuple-element.41, f32[2,2,320]{2,1,0:T(2,128)S(1)} %get-tuple-element.40), kind=kOutput, calls=%fused_computation.56 | convolution fusion | flops 107890240 | bytes 3937280 | tf_op jit(solution)/shard_map/bhqk,bqhd->bkhd/dot_general | solution.py:32
  30.9 3.8 %fusion.81 = bf16[2,320,2,128]{3,1,2,0:T(8,128)(2,1)} fusion(f32[2,2,320,320]{2,3,1,0:T(8,128)S(1)} %fusion.133, bf16[2,320,2,128]{3,2,1,0:T(2,128)(2,1)} %copy-done.22, f32[2,2,320,320]{2,3,1,0:T(8,128)} %get-tuple-element.39, f32[2,2,320]{2,1,0:T(2,128)S(1)} %get-tuple-element.38), kind=kOutput, calls=%fused_computation.59 | convolution fusion | flops 107890240 | bytes 3937280 | tf_op jit(solution)/shard_map/bhqk,bkhd->bqhd/dot_general | solution.py:31
  34.7 3.6 %fusion.78 = bf16[2,320,2,128]{3,1,2,0:T(8,128)(2,1)} fusion(f32[2,2,320,320]{2,3,1,0:T(8,128)S(1)} %fusion.133, bf16[2,320,2,128]{3,2,1,0:T(2,128)(2,1)} %copy-done.20, f32[2,2,320,320]{2,3,1,0:T(8,128)} %get-tuple-element.39, f32[2,2,320]{2,1,0:T(2,128)S(1)} %get-tuple-element.38), kind=kOutput, calls=%fused_computation.58 | convolution fusion | flops 107890240 | bytes 3937280 | tf_op jit(solution)/shard_map/bhqk,bqhd->bkhd/dot_general | solution.py:32
  38.3 2.8 %fusion.97 = bf16[2,320,2,128]{3,1,2,0:T(8,128)(2,1)} fusion(bf16[2,320,2,128]{3,2,1,0:T(2,128)(2,1)} %reshape.150, f32[2,2,320,320]{2,3,1,0:T(8,128)} %get-tuple-element.39, f32[2,2,320]{2,1,0:T(2,128)S(1)} %get-tuple-element.38), kind=kOutput, calls=%fused_computation.65 | convolution fusion | flops 105840640 | bytes 2298880 | tf_op jit(solution)/shard_map/bhqk,bqhd->bkhd/dot_general | solution.py:27
  46.6 3.8 %fusion.87 = bf16[2,320,2,128]{3,1,2,0:T(8,128)(2,1)} fusion(f32[2,2,320,320]{2,3,1,0:T(8,128)S(1)} %fusion.131, bf16[2,320,2,128]{3,2,1,0:T(2,128)(2,1)} %copy-done.23, f32[2,2,320,320]{2,3,1,0:T(8,128)} %get-tuple-element.37, f32[2,2,320]{2,1,0:T(2,128)S(1)} %get-tuple-element.36), kind=kOutput, calls=%fused_computation.61 | convolution fusion | flops 107890240 | bytes 3937280 | tf_op jit(solution)/shard_map/bhqk,bkhd->bqhd/dot_general | solution.py:31
  50.4 3.6 %fusion.84 = bf16[2,320,2,128]{3,1,2,0:T(8,128)(2,1)} fusion(f32[2,2,320,320]{2,3,1,0:T(8,128)S(1)} %fusion.131, bf16[2,320,2,128]{3,2,1,0:T(2,128)(2,1)} %copy-done.21, f32[2,2,320,320]{2,3,1,0:T(8,128)} %get-tuple-element.37, f32[2,2,320]{2,1,0:T(2,128)S(1)} %get-tuple-element.36), kind=kOutput, calls=%fused_computation.60 | convolution fusion | flops 107890240 | bytes 3937280 | tf_op jit(solution)/shard_map/bhqk,bqhd->bkhd/dot_general | solution.py:32
  59.8 3.6 %fusion.90 = bf16[2,320,2,128]{3,1,2,0:T(8,128)(2,1)} fusion(f32[2,2,320,320]{2,3,1,0:T(8,128)S(1)} %fusion.129, bf16[2,320,2,128]{3,2,1,0:T(2,128)(2,1)S(1)} %reshape.156, f32[2,2,320,320]{2,3,1,0:T(8,128)} %get-tuple-element.35, f32[2,2,320]{2,1,0:T(2,128)S(1)} %get-tuple-element.34), kind=kOutput, calls=%fused_computation.62 | convolution fusion | flops 107890240 | bytes 3937280 | tf_op jit(solution)/shard_map/bhqk,bqhd->bkhd/dot_general | solution.py:32
  63.4 3.7 %fusion.93 = bf16[2,320,2,128]{3,1,2,0:T(8,128)(2,1)} fusion(f32[2,2,320,320]{2,3,1,0:T(8,128)S(1)} %fusion.129, bf16[2,320,2,128]{3,2,1,0:T(2,128)(2,1)S(1)} %reshape.157, f32[2,2,320,320]{2,3,1,0:T(8,128)} %get-tuple-element.35, f32[2,2,320]{2,1,0:T(2,128)S(1)} %get-tuple-element.34), kind=kOutput, calls=%fused_computation.63 | convolution fusion | flops 107890240 | bytes 3937280 | tf_op jit(solution)/shard_map/bhqk,bkhd->bqhd/dot_general | solution.py:31
  99.6 22.9 %all_gather.7 = f32[16,3,4096]{2,1,0:T(4,128)} all-gather(f32[1,3,4096]{2,1,0:T(4,128)S(1)} %fusion.197), channel_id=1, replica_groups=mesh['section'=2,'dp'=4,'mp'=4] {'dp','mp'}, dimensions={0}, use_global_device_ids=true | all-gather | bytes 835584 | tf_op jit(solution)/shard_map/all_gather | solution.py:87
  137.4 3.9 %collective-permute-done.1 = bf16[3,160,256]{2,1,0:T(8,128)(2,1)} collective-permute-done((bf16[3,160,256]{2,1,0:T(8,128)(2,1)}, bf16[3,160,256]{2,1,0:T(8,128)(2,1)}, u32[]{:S(2)}, u32[]{:S(2)}) %collective-permute-start.1) | collective-permute-done | bytes 245792 | tf_op jit(solution)/shard_map/ppermute | solution.py:82
  142.6 3.9 %collective-permute-done.2 = bf16[3,160,256]{2,1,0:T(8,128)(2,1)S(1)} collective-permute-done((bf16[3,160,256]{2,1,0:T(8,128)(2,1)}, bf16[3,160,256]{2,1,0:T(8,128)(2,1)S(1)}, u32[]{:S(2)}, u32[]{:S(2)}) %collective-permute-start.2) | collective-permute-done | bytes 245792 | tf_op jit(solution)/shard_map/ppermute | solution.py:82
  147.7 4.0 %collective-permute-done.3 = bf16[3,160,256]{2,1,0:T(8,128)(2,1)S(1)} collective-permute-done((bf16[3,160,256]{2,1,0:T(8,128)(2,1)}, bf16[3,160,256]{2,1,0:T(8,128)(2,1)S(1)}, u32[]{:S(2)}, u32[]{:S(2)}) %collective-permute-start.3) | collective-permute-done | bytes 245792 | tf_op jit(solution)/shard_map/ppermute | solution.py:82
  153.0 5.1 %collective-permute-done.4 = bf16[3,160,256]{2,1,0:T(8,128)(2,1)S(1)} collective-permute-done((bf16[3,160,256]{2,1,0:T(8,128)(2,1)}, bf16[3,160,256]{2,1,0:T(8,128)(2,1)S(1)}, u32[]{:S(2)}, u32[]{:S(2)}) %collective-permute-start.4) | collective-permute-done | bytes 245792 | tf_op jit(solution)/shard_map/ppermute | solution.py:82
  159.4 4.0 %collective-permute-done.5 = bf16[3,160,256]{2,1,0:T(8,128)(2,1)S(1)} collective-permute-done((bf16[3,160,256]{2,1,0:T(8,128)(2,1)}, bf16[3,160,256]{2,1,0:T(8,128)(2,1)S(1)}, u32[]{:S(2)}, u32[]{:S(2)}) %collective-permute-start.5) | collective-permute-done | bytes 245792 | tf_op jit(solution)/shard_map/ppermute | solution.py:82
  175.2 6.5 %collective-permute-done.8 = bf16[3,160,256]{2,1,0:T(8,128)(2,1)S(1)} collective-permute-done((bf16[3,160,256]{2,1,0:T(8,128)(2,1)S(1)}, bf16[3,160,256]{2,1,0:T(8,128)(2,1)S(1)}, u32[]{:S(2)}, u32[]{:S(2)}) %collective-permute-start.8) | collective-permute-done | bytes 245792 | tf_op jit(solution)/shard_map/ppermute | solution.py:82
  183.0 4.0 %collective-permute-done.9 = bf16[3,160,256]{2,1,0:T(8,128)(2,1)S(1)} collective-permute-done((bf16[3,160,256]{2,1,0:T(8,128)(2,1)S(1)}, bf16[3,160,256]{2,1,0:T(8,128)(2,1)S(1)}, u32[]{:S(2)}, u32[]{:S(2)}) %collective-permute-start.9) | collective-permute-done | bytes 245792 | tf_op jit(solution)/shard_map/ppermute | solution.py:82
  188.2 4.0 %collective-permute-done.10 = bf16[3,160,256]{2,1,0:T(8,128)(2,1)S(1)} collective-permute-done((bf16[3,160,256]{2,1,0:T(8,128)(2,1)S(1)}, bf16[3,160,256]{2,1,0:T(8,128)(2,1)S(1)}, u32[]{:S(2)}, u32[]{:S(2)}) %collective-permute-start.10) | collective-permute-done | bytes 245792 | tf_op jit(solution)/shard_map/ppermute | solution.py:82
  193.6 3.9 %collective-permute-done.11 = bf16[3,160,256]{2,1,0:T(8,128)(2,1)S(1)} collective-permute-done((bf16[3,160,256]{2,1,0:T(8,128)(2,1)S(1)}, bf16[3,160,256]{2,1,0:T(8,128)(2,1)S(1)}, u32[]{:S(2)}, u32[]{:S(2)}) %collective-permute-start.11) | collective-permute-done | bytes 245792 | tf_op jit(solution)/shard_map/ppermute | solution.py:82
  197.6 6.0 %collective-permute-done.12 = bf16[3,160,256]{2,1,0:T(8,128)(2,1)S(1)} collective-permute-done((bf16[3,160,256]{2,1,0:T(8,128)(2,1)S(1)}, bf16[3,160,256]{2,1,0:T(8,128)(2,1)S(1)}, u32[]{:S(2)}, u32[]{:S(2)}) %collective-permute-start.12) | collective-permute-done | bytes 245792 | tf_op jit(solution)/shard_map/ppermute | solution.py:82
  203.6 5.3 %collective-permute-done.13 = bf16[3,160,256]{2,1,0:T(8,128)(2,1)S(1)} collective-permute-done((bf16[3,160,256]{2,1,0:T(8,128)(2,1)S(1)}, bf16[3,160,256]{2,1,0:T(8,128)(2,1)S(1)}, u32[]{:S(2)}, u32[]{:S(2)}) %collective-permute-start.13) | collective-permute-done | bytes 245792 | tf_op jit(solution)/shard_map/ppermute | solution.py:82
  208.8 5.3 %collective-permute-done.14 = bf16[3,160,256]{2,1,0:T(8,128)(2,1)S(1)} collective-permute-done((bf16[3,160,256]{2,1,0:T(8,128)(2,1)S(1)}, bf16[3,160,256]{2,1,0:T(8,128)(2,1)S(1)}, u32[]{:S(2)}, u32[]{:S(2)}) %collective-permute-start.14) | collective-permute-done | bytes 245792 | tf_op jit(solution)/shard_map/ppermute | solution.py:82
  214.1 4.7 %collective-permute-done.15 = bf16[3,160,256]{2,1,0:T(8,128)(2,1)S(1)} collective-permute-done((bf16[3,160,256]{2,1,0:T(8,128)(2,1)S(1)}, bf16[3,160,256]{2,1,0:T(8,128)(2,1)S(1)}, u32[]{:S(2)}, u32[]{:S(2)}) %collective-permute-start.15) | collective-permute-done | bytes 245792 | tf_op jit(solution)/shard_map/ppermute | solution.py:82
  (164 shorter events, 100.7 us)
Async XLA Ops:
  0.6 3.2 %copy-start.10 = (bf16[1,1,640,1024]{3,2,1,0:T(8,128)(2,1)S(1)}, bf16[1,1,640,1024]{3,2,1,0:T(8,128)(2,1)}, u32[]{:S(2)}) copy-start(bf16[1,1,640,1024]{3,2,1,0:T(8,128)(2,1)} %param.6) | copy-start | bytes 3932164
  4.8 3.9 %copy-start.11 = (bf16[1,1,640,1024]{3,2,1,0:T(8,128)(2,1)S(1)}, bf16[1,1,640,1024]{3,2,1,0:T(8,128)(2,1)}, u32[]{:S(2)}) copy-start(bf16[1,1,640,1024]{3,2,1,0:T(8,128)(2,1)} %param.7) | copy-start | bytes 3932164
  22.7 3.0 %copy-start.8 = (bf16[640,256]{1,0:T(8,128)(2,1)S(1)}, bf16[640,256]{1,0:T(8,128)(2,1)}, u32[]{:S(2)}) copy-start(bf16[640,256]{1,0:T(8,128)(2,1)} %get-tuple-element.13) | copy-start | bytes 983044
  38.3 3.0 %copy-start.4 = (bf16[640,256]{1,0:T(8,128)(2,1)S(1)}, bf16[640,256]{1,0:T(8,128)(2,1)}, u32[]{:S(2)}) copy-start(bf16[640,256]{1,0:T(8,128)(2,1)} %get-tuple-element.12) | copy-start | bytes 983044
  123.8 10.3 %collective-permute-start.16 = (f32[3,4096]{1,0:T(4,128)S(1)}, f32[3,4096]{1,0:T(4,128)}, u32[]{:S(2)}, u32[]{:S(2)}) collective-permute-start(f32[3,4096]{1,0:T(4,128)S(1)} %reduce_sum.129), channel_id=1, source_target_pairs={{16,0},{17,1},{18,2},{19,3},{20,4},{21,5},{22,6},{23,7},{24,8},{25... | collective-permute-start | bytes 147464 | tf_op jit(solution)/shard_map/ppermute | solution.py:88
  126.0 6.0 %copy-start = (bf16[3,640,256]{2,1,0:T(8,128)(2,1)S(1)}, bf16[3,640,256]{2,1,0:T(8,128)(2,1)}, u32[]{:S(2)}) copy-start(bf16[3,640,256]{2,1,0:T(8,128)(2,1)} %constant_dynamic-update-slice_fusion.9) | copy-start | bytes 2949124
  126.0 10.1 %collective-permute-start = (bf16[3,160,256]{2,1,0:T(8,128)(2,1)S(1)}, bf16[3,160,256]{2,1,0:T(8,128)(2,1)}, u32[]{:S(2)}, u32[]{:S(2)}) collective-permute-start(bf16[3,160,256]{2,1,0:T(8,128)(2,1)S(1)} %get-tuple-element.21), channel_id=1, source_target_pairs={{16,0},{17,1},{18,2},{19,3},{20,4},{21,5},{22,6},{23,7},{24,8},{25... | collective-permute-start | bytes 737288 | tf_op jit(solution)/shard_map/ppermute | solution.py:82
  128.3 29.8 %copy-start.24 = (bf16[3,160,256]{2,1,0:T(8,128)(2,1)S(1)}, bf16[3,160,256]{2,1,0:T(8,128)(2,1)}, u32[]{:S(2)}) copy-start(bf16[3,160,256]{2,1,0:T(8,128)(2,1)} %get-tuple-element.23) | copy-start | bytes 737284
  128.3 13.0 %collective-permute-start.1 = (bf16[3,160,256]{2,1,0:T(8,128)(2,1)}, bf16[3,160,256]{2,1,0:T(8,128)(2,1)}, u32[]{:S(2)}, u32[]{:S(2)}) collective-permute-start(bf16[3,160,256]{2,1,0:T(8,128)(2,1)} %get-tuple-element.25), channel_id=1, source_target_pairs={{16,0},{17,1},{18,2},{19,3},{20,4},{21,5},{22,6},{23,7},{24,8},{25... | collective-permute-start | bytes 737288 | tf_op jit(solution)/shard_map/ppermute | solution.py:82
  130.6 10.7 %copy-start.25 = (bf16[3,160,256]{2,1,0:T(8,128)(2,1)S(1)}, bf16[3,160,256]{2,1,0:T(8,128)(2,1)}, u32[]{:S(2)}) copy-start(bf16[3,160,256]{2,1,0:T(8,128)(2,1)} %get-tuple-element.28) | copy-start | bytes 737284
  130.6 15.9 %collective-permute-start.2 = (bf16[3,160,256]{2,1,0:T(8,128)(2,1)}, bf16[3,160,256]{2,1,0:T(8,128)(2,1)S(1)}, u32[]{:S(2)}, u32[]{:S(2)}) collective-permute-start(bf16[3,160,256]{2,1,0:T(8,128)(2,1)} %get-tuple-element.29), channel_id=1, source_target_pairs={{16,0},{17,1},{18,2},{19,3},{20,4},{21,5},{22,6},{23,7},{24,8},{25... | collective-permute-start | bytes 737288 | tf_op jit(solution)/shard_map/ppermute | solution.py:82
  132.8 18.9 %collective-permute-start.3 = (bf16[3,160,256]{2,1,0:T(8,128)(2,1)}, bf16[3,160,256]{2,1,0:T(8,128)(2,1)S(1)}, u32[]{:S(2)}, u32[]{:S(2)}) collective-permute-start(bf16[3,160,256]{2,1,0:T(8,128)(2,1)} %get-tuple-element.33), channel_id=1, source_target_pairs={{16,0},{17,1},{18,2},{19,3},{20,4},{21,5},{22,6},{23,7},{24,8},{25... | collective-permute-start | bytes 737288 | tf_op jit(solution)/shard_map/ppermute | solution.py:82
  134.1 24.0 %collective-permute-start.4 = (bf16[3,160,256]{2,1,0:T(8,128)(2,1)}, bf16[3,160,256]{2,1,0:T(8,128)(2,1)S(1)}, u32[]{:S(2)}, u32[]{:S(2)}) collective-permute-start(bf16[3,160,256]{2,1,0:T(8,128)(2,1)} %get-tuple-element.20), channel_id=1, source_target_pairs={{16,1},{17,2},{18,3},{19,0},{20,5},{21,6},{22,7},{23,4},{24,9},{25... | collective-permute-start | bytes 737288 | tf_op jit(solution)/shard_map/ppermute | solution.py:82
  136.0 27.4 %collective-permute-start.5 = (bf16[3,160,256]{2,1,0:T(8,128)(2,1)}, bf16[3,160,256]{2,1,0:T(8,128)(2,1)S(1)}, u32[]{:S(2)}, u32[]{:S(2)}) collective-permute-start(bf16[3,160,256]{2,1,0:T(8,128)(2,1)} %get-tuple-element.24), channel_id=1, source_target_pairs={{16,1},{17,2},{18,3},{19,0},{20,5},{21,6},{22,7},{23,4},{24,9},{25... | collective-permute-start | bytes 737288 | tf_op jit(solution)/shard_map/ppermute | solution.py:82
  141.3 27.3 %collective-permute-start.6 = (bf16[3,160,256]{2,1,0:T(8,128)(2,1)S(1)}, bf16[3,160,256]{2,1,0:T(8,128)(2,1)S(1)}, u32[]{:S(2)}, u32[]{:S(2)}) collective-permute-start(bf16[3,160,256]{2,1,0:T(8,128)(2,1)S(1)} %copy-done.25), channel_id=1, source_target_pairs={{16,1},{17,2},{18,3},{19,0},{20,5},{21,6},{22,7},{23,4},{24,9},{25... | collective-permute-start | bytes 737288 | tf_op jit(solution)/shard_map/ppermute | solution.py:82
  146.5 27.5 %collective-permute-start.7 = (bf16[3,160,256]{2,1,0:T(8,128)(2,1)S(1)}, bf16[3,160,256]{2,1,0:T(8,128)(2,1)S(1)}, u32[]{:S(2)}, u32[]{:S(2)}) collective-permute-start(bf16[3,160,256]{2,1,0:T(8,128)(2,1)S(1)} %get-tuple-element.32), channel_id=1, source_target_pairs={{16,1},{17,2},{18,3},{19,0},{20,5},{21,6},{22,7},{23,4},{24,9},{25... | collective-permute-start | bytes 737288 | tf_op jit(solution)/shard_map/ppermute | solution.py:82
  151.7 29.9 %collective-permute-start.8 = (bf16[3,160,256]{2,1,0:T(8,128)(2,1)S(1)}, bf16[3,160,256]{2,1,0:T(8,128)(2,1)S(1)}, u32[]{:S(2)}, u32[]{:S(2)}) collective-permute-start(bf16[3,160,256]{2,1,0:T(8,128)(2,1)S(1)} %get-tuple-element.19), channel_id=1, source_target_pairs={{16,2},{17,3},{18,0},{19,1},{20,6},{21,7},{22,4},{23,5},{24,10},{2... | collective-permute-start | bytes 737288 | tf_op jit(solution)/shard_map/ppermute | solution.py:82
  158.1 28.8 %collective-permute-start.9 = (bf16[3,160,256]{2,1,0:T(8,128)(2,1)S(1)}, bf16[3,160,256]{2,1,0:T(8,128)(2,1)S(1)}, u32[]{:S(2)}, u32[]{:S(2)}) collective-permute-start(bf16[3,160,256]{2,1,0:T(8,128)(2,1)S(1)} %copy-done.24), channel_id=1, source_target_pairs={{16,2},{17,3},{18,0},{19,1},{20,6},{21,7},{22,4},{23,5},{24,10},{2... | collective-permute-start | bytes 737288 | tf_op jit(solution)/shard_map/ppermute | solution.py:82
  163.4 28.8 %collective-permute-start.10 = (bf16[3,160,256]{2,1,0:T(8,128)(2,1)S(1)}, bf16[3,160,256]{2,1,0:T(8,128)(2,1)S(1)}, u32[]{:S(2)}, u32[]{:S(2)}) collective-permute-start(bf16[3,160,256]{2,1,0:T(8,128)(2,1)S(1)} %get-tuple-element.27), channel_id=1, source_target_pairs={{16,2},{17,3},{18,0},{19,1},{20,6},{21,7},{22,4},{23,5},{24,10},{2... | collective-permute-start | bytes 737288 | tf_op jit(solution)/shard_map/ppermute | solution.py:82
  168.7 28.8 %collective-permute-start.11 = (bf16[3,160,256]{2,1,0:T(8,128)(2,1)S(1)}, bf16[3,160,256]{2,1,0:T(8,128)(2,1)S(1)}, u32[]{:S(2)}, u32[]{:S(2)}) collective-permute-start(bf16[3,160,256]{2,1,0:T(8,128)(2,1)S(1)} %get-tuple-element.31), channel_id=1, source_target_pairs={{16,2},{17,3},{18,0},{19,1},{20,6},{21,7},{22,4},{23,5},{24,10},{2... | collective-permute-start | bytes 737288 | tf_op jit(solution)/shard_map/ppermute | solution.py:82
  173.9 29.7 %collective-permute-start.12 = (bf16[3,160,256]{2,1,0:T(8,128)(2,1)S(1)}, bf16[3,160,256]{2,1,0:T(8,128)(2,1)S(1)}, u32[]{:S(2)}, u32[]{:S(2)}) collective-permute-start(bf16[3,160,256]{2,1,0:T(8,128)(2,1)S(1)} %get-tuple-element.18), channel_id=1, source_target_pairs={{16,3},{17,0},{18,1},{19,2},{20,7},{21,4},{22,5},{23,6},{24,11},{2... | collective-permute-start | bytes 737288 | tf_op jit(solution)/shard_map/ppermute | solution.py:82
  181.7 27.2 %collective-permute-start.13 = (bf16[3,160,256]{2,1,0:T(8,128)(2,1)S(1)}, bf16[3,160,256]{2,1,0:T(8,128)(2,1)S(1)}, u32[]{:S(2)}, u32[]{:S(2)}) collective-permute-start(bf16[3,160,256]{2,1,0:T(8,128)(2,1)S(1)} %get-tuple-element.22), channel_id=1, source_target_pairs={{16,3},{17,0},{18,1},{19,2},{20,7},{21,4},{22,5},{23,6},{24,11},{2... | collective-permute-start | bytes 737288 | tf_op jit(solution)/shard_map/ppermute | solution.py:82
  186.9 27.2 %collective-permute-start.14 = (bf16[3,160,256]{2,1,0:T(8,128)(2,1)S(1)}, bf16[3,160,256]{2,1,0:T(8,128)(2,1)S(1)}, u32[]{:S(2)}, u32[]{:S(2)}) collective-permute-start(bf16[3,160,256]{2,1,0:T(8,128)(2,1)S(1)} %get-tuple-element.26), channel_id=1, source_target_pairs={{16,3},{17,0},{18,1},{19,2},{20,7},{21,4},{22,5},{23,6},{24,11},{2... | collective-permute-start | bytes 737288 | tf_op jit(solution)/shard_map/ppermute | solution.py:82
  192.2 26.6 %collective-permute-start.15 = (bf16[3,160,256]{2,1,0:T(8,128)(2,1)S(1)}, bf16[3,160,256]{2,1,0:T(8,128)(2,1)S(1)}, u32[]{:S(2)}, u32[]{:S(2)}) collective-permute-start(bf16[3,160,256]{2,1,0:T(8,128)(2,1)S(1)} %get-tuple-element.30), channel_id=1, source_target_pairs={{16,3},{17,0},{18,1},{19,2},{20,7},{21,4},{22,5},{23,6},{24,11},{2... | collective-permute-start | bytes 737288 | tf_op jit(solution)/shard_map/ppermute | solution.py:82
  (20 other events, 35.7 us)
